TPU v7x, 128 devices: a whole 4x4x4 slice. The times are simulated.
128 devices in a mesh: dp: 4 (over x), tensor: 32 (over z, y, core).
Axes of the slice: x: 4, y: 4, z: 4, core: 2. Of those that a mesh axis runs over, the one named last changes fastest.
Arguments:
- inputs: bfloat16 [1024, 28672], P('dp', 'tensor'), may hold values from -0.1875 to 0.1875
- output_gradient: bfloat16 [1024, 8192], P('dp', 'tensor'), may hold values from -6 to 6
- frozen: bfloat16 [8192, 28672], P('dp', 'tensor'), may hold values from -0.5905695 to 0.5905695
- adapter_down_factor: bfloat16 [64, 28672], P(None, 'tensor'), may hold values from -0.03125 to 0.03125
- adapter_up_factor: bfloat16 [8192, 64], P('dp'), may hold values from -0.3125 to 0.3125
- magnitude: float32 [8192], P('dp'), may hold values from 0.5 to 2
Outputs:
- input_gradient_rows: bfloat16 [1024, 28672], P('dp', 'tensor')
- adapter_down_gradient: float32 [64, 28672], P(None, 'tensor')
- adapter_up_gradient: float32 [8192, 64], P('dp')
- magnitude_gradient: float32 [8192], P('dp')
All inputs are finite; a program needn't handle non-finite values.
Results may differ from a plain program's by a relative error of at most 0.0057.
Values may be sent and summed in bfloat16 or wider, within the bound.
No kernel may reach another device: no remote copies, remote signals or barrier semaphores. Data moves between devices by JAX's collectives and lax.ppermute only.
A program may use at most 128 MiB of HBM per device.

v0:
```python
import jax
import jax.numpy as jnp
from jax import lax
from jax.sharding import PartitionSpec as P

adapter_scale = 2.0
epsilon = 1e-06


def local(inputs, output_gradient, frozen, adapter_down_factor, adapter_up_factor, magnitude):
    full_grad = lax.all_gather(output_gradient, "tensor", axis=1, tiled=True)
    row_grad = lax.all_to_all(full_grad, "dp", split_axis=1, concat_axis=0, tiled=True)
    combined_weight = frozen.astype(jnp.float32) + adapter_scale * jnp.dot(
        adapter_up_factor, adapter_down_factor, preferred_element_type=jnp.float32
    )
    merged_b = combined_weight.astype(jnp.bfloat16)
    squares = jnp.sum(combined_weight * combined_weight, axis=1)
    total_squares = lax.psum(squares, "tensor")
    weight_row_norm = jnp.sqrt(total_squares + epsilon)
    col_scale = magnitude / weight_row_norm
    scaled_rows = (row_grad.astype(jnp.float32) * col_scale[None, :]).astype(jnp.bfloat16)
    summed = lax.psum_scatter(
        jnp.dot(scaled_rows, merged_b, preferred_element_type=jnp.float32),
        "dp",
        scatter_dimension=0,
        tiled=True,
    )
    input_gradient_rows = summed.astype(jnp.bfloat16)
    product = lax.dot_general(
        row_grad,
        lax.all_gather(inputs, "dp", axis=0, tiled=True),
        (((0,), (0,)), ((), ())),
        preferred_element_type=jnp.float32,
    )
    gradient_row_sums = lax.psum(jnp.sum(product * combined_weight, axis=1), "tensor")
    combined_weight_gradient = col_scale[:, None] * product
    down_partial_sum = adapter_scale * lax.dot_general(
        adapter_up_factor.astype(jnp.float32),
        combined_weight_gradient,
        (((0,), (0,)), ((), ())),
        precision=lax.Precision.HIGHEST,
    )
    adapter_down_gradient = lax.psum(down_partial_sum, "dp")
    up_partial_sum = adapter_scale * jnp.dot(
        combined_weight_gradient,
        adapter_down_factor.astype(jnp.float32).T,
        precision=lax.Precision.HIGHEST,
    )
    adapter_up_gradient = lax.psum(up_partial_sum, "tensor")
    magnitude_gradient = gradient_row_sums / weight_row_norm
    return (input_gradient_rows, adapter_down_gradient, adapter_up_gradient, magnitude_gradient)


def solution(mesh):
    placed = (
        P("dp", "tensor"),
        P("dp", "tensor"),
        P("dp", "tensor"),
        P(None, "tensor"),
        P("dp", None),
        P("dp"),
    )
    return jax.shard_map(
        local,
        mesh=mesh,
        in_specs=placed,
        out_specs=(P("dp", "tensor"), P(None, "tensor"), P("dp", None), P("dp")),
        check_vma=False,
    )
```

profile of v0, /device:TPU:1, one launch (start us, length us, event | category | flops | bytes accessed | tf_op | source)
XLA Modules:
  0.0 486.6 jit_solution(599287304383377299)
XLA Ops:
  8.0 0.0 copy-start
  8.0 0.0 all-gather.3.cloned.1.call-start
  8.1 1.7 copy.12
  9.8 0.0 all-gather.3.cloned.1.call-update
  9.8 51.7 %all-gather.3.cloned.1.call-done = bf16[256,8192]{0,1:T(8,128)(2,1)} async-done(((bf16[256,256]{0,1:T(8,128)(2,1)}), bf16[256,8192]{0,1:T(8,128)(2,1)}) %all-gather.3.cloned.1.call-update) | async-done | bytes 4194320 | tf_op jit(solution)/shard_map/all_gather | solution.py:11
  61.5 5.0 %all-to-all-start = ((bf16[256,4,2048]{0,2,1:T(8,128)(2,1)}), bf16[256,4,2048]{0,2,1:T(8,128)(2,1)}, u32[]{:S(2)}, u32[]{:S(2)}) async-start(bf16[256,4,2048]{0,2,1:T(8,128)(2,1)} %bitcast.11), calls=%async_computation | async-start | bytes 8388608 | tf_op jit(solution)/shard_map/all_to_all | solution.py:12
  66.5 0.0 all-gather.5.cloned.1.call-start
  66.5 0.5 all-gather.5.cloned.1.call-update
  67.1 0.0 reduce-scatter.2.cloned.1.call-start
  67.1 6.2 %copy.14 = bf16[2048,896]{0,1:T(8,128)(2,1)} copy(bf16[2048,896]{1,0:T(8,128)(2,1)} %param.8) | data formatting | bytes 7340032 | tf_op args[2]
  73.3 0.0 copy-done
  73.3 0.0 copy-done.1
  73.3 6.1 %multiply_add_fusion = f32[2048,896]{0,1:T(8,128)} fusion(bf16[2048,896]{0,1:T(8,128)(2,1)} %copy.14, bf16[2048,64]{0,1:T(8,128)(2,1)S(1)} %copy-done, bf16[64,896]{1,0:T(8,128)(2,1)S(1)} %copy-done.1), kind=kOutput, calls=%fused_computation.3 | convolution fusion | flops 240386048 | bytes 11386880 | tf_op jit(solution)/shard_map/dot_general | solution.py:13
  79.4 50.5 %all-to-all-done = bf16[256,4,2048]{0,2,1:T(8,128)(2,1)} async-done(((bf16[256,4,2048]{0,2,1:T(8,128)(2,1)}), bf16[256,4,2048]{0,2,1:T(8,128)(2,1)}, u32[]{:S(2)}, u32[]{:S(2)}) %all-to-all-start) | async-done | bytes 4194336 | tf_op jit(solution)/shard_map/all_to_all | solution.py:12
  129.9 6.3 %copy.13 = bf16[4,256,2048]{2,1,0:T(8,128)(2,1)} copy(bf16[4,256,2048]{1,2,0:T(8,128)(2,1)} %bitcast.1) | data formatting | bytes 8388608 | tf_op jit(solution)/shard_map/all_to_all | solution.py:12
  136.2 12.5 %multiply_reduce_fusion = (f32[2048]{0:T(1024)S(1)}, f32[2048]{0:T(1024)S(1)}, f32[2048,896]{0,1:T(8,128)}) fusion(f32[2048,896]{0,1:T(8,128)} %multiply_add_fusion, bf16[1024,2048]{1,0:T(8,128)(2,1)} %bitcast.12, bf16[1024,896]{1,0:T(8,128)(2,1)} %all-gather.5.cloned.1.call-done), kind=kOutput, calls=%fused_computation.1 | convolution fusion | flops 3765432320 | bytes 20725760 | tf_op jit(solution)/shard_map/dot_general | solution.py:29
  148.7 120.9 %all-reduce = (f32[2048]{0:T(1024)S(1)}, f32[2048]{0:T(1024)S(1)}) all-reduce(f32[2048]{0:T(1024)S(1)} %get-tuple-element.5, f32[2048]{0:T(1024)S(1)} %get-tuple-element.4), channel_id=1, replica_groups=mesh['dp'=4,'tensor'=32] {'tensor'}, use_global_device_ids=true, to_apply=%region_1.0 | all-reduce | flops 4096 | bytes 32768 | tf_op jit(solution)/shard_map/psum | solution.py:18
  269.6 0.6 fusion.18
  270.2 10.7 %fusion.4 = f32[1024,896]{1,0:T(8,128)} fusion(bf16[1024,2048]{1,0:T(8,128)(2,1)} %bitcast.13, f32[2048]{0:T(1024)S(1)} %get-tuple-element.9, f32[2048,896]{0,1:T(8,128)} %multiply_add_fusion), kind=kOutput, calls=%fused_computation.8 | convolution fusion | flops 3766222848 | bytes 15212544 | tf_op jit(solution)/shard_map/dot_general | solution.py:23
  280.9 0.0 reduce-scatter.2.cloned.1.call-update
  281.0 0.2 all-reduce.4.cloned.1.call-start
  281.2 7.8 %fusion.15 = f32[64,896]{1,0:T(8,128)} fusion(bf16[2048,64]{0,1:T(8,128)(2,1)S(1)} %copy-done, f32[2048,896]{0,1:T(8,128)} %get-tuple-element.10, f32[2048]{0:T(1024)S(1)} %get-tuple-element.9), kind=kOutput, calls=%fused_computation.15 | convolution fusion | flops 1411178496 | bytes 7839744 | tf_op jit(solution)/shard_map/dot_general | solution.py:37
  289.0 0.0 all-reduce.4.cloned.1.call-update
  289.0 0.0 all-reduce.6.cloned.1.call-start
  289.1 7.4 %fusion.9 = f32[2048,64]{0,1:T(8,128)} fusion(bf16[64,896]{1,0:T(8,128)(2,1)S(1)} %copy-done.1, f32[2048,896]{0,1:T(8,128)} %get-tuple-element.10, f32[2048]{0:T(1024)S(1)} %get-tuple-element.9), kind=kOutput, calls=%fused_computation.13 | convolution fusion | flops 1411252224 | bytes 7987200 | tf_op jit(solution)/shard_map/dot_general | solution.py:44
  296.4 0.0 all-reduce.6.cloned.1.call-update
  296.5 26.3 %reduce-scatter.2.cloned.1.call-done = f32[256,896]{1,0:T(8,128)} async-done(((f32[1024,896]{1,0:T(8,128)}), f32[256,896]{1,0:T(8,128)}) %reduce-scatter.2.cloned.1.call-update) | async-done | bytes 917520 | tf_op jit(solution)/shard_map/reduce_scatter | solution.py:22
  322.8 2.0 convert_element_type.21
  324.8 40.2 %all-reduce.4.cloned.1.call-done = f32[64,896]{1,0:T(8,128)} async-done(((f32[64,896]{1,0:T(8,128)}), f32[64,896]{1,0:T(8,128)}) %all-reduce.4.cloned.1.call-update) | async-done | bytes 229392 | tf_op jit(solution)/shard_map/psum | solution.py:43
  365.0 110.5 %all-reduce.6.cloned.1.call-done = f32[2048,64]{0,1:T(8,128)} async-done(((f32[2048,64]{0,1:T(8,128)}), f32[2048,64]{0,1:T(8,128)}) %all-reduce.6.cloned.1.call-update) | async-done | bytes 524304 | tf_op jit(solution)/shard_map/psum | solution.py:49
  475.4 1.6 copy.17
  477.1 1.9 copy.18
  (4 shorter events, 0.0 us)
Async XLA Ops:
  8.0 65.3 %copy-start = (bf16[2048,64]{0,1:T(8,128)(2,1)S(1)}, bf16[2048,64]{0,1:T(8,128)(2,1)}, u32[]{:S(2)}) copy-start(bf16[2048,64]{0,1:T(8,128)(2,1)} %param.10) | copy-start | bytes 786436
  8.0 53.5 %all-gather.3.cloned.1.call-start = ((), (), s32[]{:S(2)}) async-start(), calls=%async_computation.2 | async-start | bytes 4325376 | tf_op jit(solution)/shard_map/all_gather | solution.py:11
  61.5 11.8 %copy-start.1 = (bf16[64,896]{1,0:T(8,128)(2,1)S(1)}, bf16[64,896]{1,0:T(8,128)(2,1)}, u32[]{:S(2)}) copy-start(bf16[64,896]{1,0:T(8,128)(2,1)} %param.9) | copy-start | bytes 344068
  61.5 68.4 %all-to-all-start = ((bf16[256,4,2048]{0,2,1:T(8,128)(2,1)}), bf16[256,4,2048]{0,2,1:T(8,128)(2,1)}, u32[]{:S(2)}, u32[]{:S(2)}) async-start(bf16[256,4,2048]{0,2,1:T(8,128)(2,1)} %bitcast.11), calls=%async_computation | async-start | bytes 8388608 | tf_op jit(solution)/shard_map/all_to_all | solution.py:12
  66.5 69.7 %all-gather.5.cloned.1.call-start = ((), (), s32[]{:S(2)}) async-start(), calls=%async_computation.4 | async-start | bytes 2293760 | tf_op jit(solution)/shard_map/all_gather | solution.py:31
  67.1 255.7 %reduce-scatter.2.cloned.1.call-start = ((), (), s32[]{:S(2)}) async-start(), calls=%async_computation.3 | async-start | bytes 4587520 | tf_op jit(solution)/shard_map/reduce_scatter | solution.py:22
  136.2 133.4 %copy-start.2 = (f32[2048]{0:T(1024)S(1)}, f32[2048]{0:T(1024)}, u32[]{:S(2)}) copy-start(f32[2048]{0:T(1024)} %param.11) | copy-start | bytes 24580
  281.0 84.0 %all-reduce.4.cloned.1.call-start = ((), (), s32[]{:S(2)}) async-start(), calls=%async_computation.5 | async-start | bytes 458752 | tf_op jit(solution)/shard_map/psum | solution.py:43
  289.0 186.4 %all-reduce.6.cloned.1.call-start = ((), (), s32[]{:S(2)}) async-start(), calls=%async_computation.6 | async-start | bytes 1048576 | tf_op jit(solution)/shard_map/psum | solution.py:49
Sparse Core Ops, SparseCore 0:
  11.7 49.7 all-gather.2
Sparse Core Ops, SparseCore 1:
  68.6 42.3 all-gather.4
  281.1 41.7 reduce-scatter.1
  325.6 39.3 all-reduce.3
  368.8 106.6 all-reduce.5
where the time goes:
time: 487 us
  waiting for transfers between devices  280 us (57%)
  blocking collectives  121 us (25%)
  matrix products  44.6 us (9%)
  local copies, waits for them, and re-layouts  17.7 us (4%)
  between operations  15.7 us (3%)
  starting transfers between devices  5.4 us (1%)
    psum x1, blocking collectives, local(): total_squares = lax.psum(squares, 'tensor')  121 us
    psum x1, waiting for transfers between devices, local(): adapter_up_gradient = lax.psum(up_partial_sum, 'tensor')  110 us
    all_gather x1, waiting for transfers between devices, local(): full_grad = lax.all_gather(output_gradient, 'tensor', axis=1, tiled=True)  51.7 us
    all_to_all x1, waiting for transfers between devices, local(): lax.all_to_all(full_grad, 'dp', split_axis=1, concat_axis=0, tiled=True)  50.5 us
    psum x1, waiting for transfers between devices, local(): adapter_down_gradient = lax.psum(down_partial_sum, 'dp')  40.2 us
    reduce_scatter x1, waiting for transfers between devices, local(): lax.psum_scatter(jnp.dot(scaled_rows, merged_b, preferred_element_type=jn...  26.3 us
    dot_general x1, matrix products, local(): lax.dot_general(row_grad, lax.all_gather(inputs, 'dp', axis=0, tiled=True...  12.5 us
    unnamed x10, local copies, waits for them, and re-layouts  11.4 us
  transfers between devices with their start and end apart: 6, of which 5 were waited for; matrix products, arithmetic and copies ran while one was open for 7% of the time, Pallas kernels for 0%

commit v1 on v0

--- a/solution.py
+++ b/solution.py
@@ -46,7 +46,7 @@
         adapter_down_factor.astype(jnp.float32).T,
         precision=lax.Precision.HIGHEST,
     )
-    adapter_up_gradient = lax.psum(up_partial_sum, "tensor")
+    adapter_up_gradient = jnp.sum(lax.all_gather(up_partial_sum, "tensor"), axis=0)
     magnitude_gradient = gradient_row_sums / weight_row_norm
     return (input_gradient_rows, adapter_down_gradient, adapter_up_gradient, magnitude_gradient)
 

time: 487 us -> 398 us (0.82)
  waiting for transfers between devices: 280 us -> 165 us
  local copies, waits for them, and re-layouts: 17.7 us -> 33.5 us
  other arithmetic: 2.61 us -> 12.2 us
    psum x1 -> x0, waiting for transfers between devices: 110 us -> none  [local(): adapter_up_gradient = lax.psum(up_partial_sum, 'tensor')]
    psum x1, waiting for transfers between devices: 40.2 us -> 0.01 us  [local(): adapter_down_gradient = lax.psum(down_partial_sum, 'dp')]
    all_gather x0 -> x1, waiting for transfers between devices: none -> 36 us  [local(): lax.all_gather(up_partial_sum, 'tensor')]
    unnamed x10, local copies, waits for them, and re-layouts: 11.4 us -> 27.2 us
    reduce_sum x0 -> x1, other arithmetic: none -> 9.55 us  [local(): jnp.sum(lax.all_gather(up_partial_sum, 'tensor'), axis=0)]
  transfers between devices with their start and end apart: 6 -> 6, of which waited for: 5 -> 4; matrix products, arithmetic and copies ran while one was open for 7% -> 16% of each run, Pallas kernels for 0% -> 0%
where the time goes in v1:
time: 398 us; the launch traced here: 397 us
  waiting for transfers between devices  165 us (41%)
  blocking collectives  121 us (30%)
  matrix products  44.8 us (11%)
  local copies, waits for them, and re-layouts  33.5 us (8%)
  between operations  15.7 us (4%)
  other arithmetic  12.2 us (3%)
  starting transfers between devices  5.4 us (1%)
    psum x1, blocking collectives, local(): total_squares = lax.psum(squares, 'tensor')  121 us
    all_gather x1, waiting for transfers between devices, local(): full_grad = lax.all_gather(output_gradient, 'tensor', axis=1, tiled=True)  51.7 us
    all_to_all x1, waiting for transfers between devices, local(): lax.all_to_all(full_grad, 'dp', split_axis=1, concat_axis=0, tiled=True)  50.5 us
    all_gather x1, waiting for transfers between devices, local(): lax.all_gather(up_partial_sum, 'tensor')  36 us
    unnamed x10, local copies, waits for them, and re-layouts  27.2 us
    reduce_scatter x1, waiting for transfers between devices, local(): lax.psum_scatter(jnp.dot(scaled_rows, merged_b, preferred_element_type=jn...  26 us
    dot_general x1, matrix products, local(): lax.dot_general(row_grad, lax.all_gather(inputs, 'dp', axis=0, tiled=True...  12.4 us
    dot_general x1, matrix products, local(): jnp.dot(scaled_rows, merged_b, preferred_element_type=jnp.float32)  10.8 us
  transfers between devices with their start and end apart: 6, of which 4 were waited for; matrix products, arithmetic and copies ran while one was open for 16% of the time, Pallas kernels for 0%

profile of v1, /device:TPU:1, one launch (start us, length us, event | category | flops | bytes accessed | tf_op | source)
XLA Modules:
  0.0 397.3 jit_solution(17612344878268518882)
XLA Ops:
  8.0 0.0 copy-start
  8.0 0.0 all-gather.5.cloned.1.call-start
  8.1 1.7 copy.12
  9.8 0.0 all-gather.5.cloned.1.call-update
  9.8 51.7 %all-gather.5.cloned.1.call-done = bf16[256,8192]{0,1:T(8,128)(2,1)} async-done(((bf16[256,256]{0,1:T(8,128)(2,1)}), bf16[256,8192]{0,1:T(8,128)(2,1)}) %all-gather.5.cloned.1.call-update) | async-done | bytes 4194320 | tf_op jit(solution)/shard_map/all_gather | solution.py:11
  61.5 5.0 %all-to-all-start = ((bf16[256,4,2048]{0,2,1:T(8,128)(2,1)}), bf16[256,4,2048]{0,2,1:T(8,128)(2,1)}, u32[]{:S(2)}, u32[]{:S(2)}) async-start(bf16[256,4,2048]{0,2,1:T(8,128)(2,1)} %bitcast.17), calls=%async_computation | async-start | bytes 8388608 | tf_op jit(solution)/shard_map/all_to_all | solution.py:12
  66.5 0.0 all-gather.7.cloned.1.call-start
  66.5 0.5 all-gather.7.cloned.1.call-update
  67.1 0.0 reduce-scatter.2.cloned.1.call-start
  67.1 6.2 %copy.14 = bf16[2048,896]{0,1:T(8,128)(2,1)} copy(bf16[2048,896]{1,0:T(8,128)(2,1)} %param.8) | data formatting | bytes 7340032 | tf_op args[2]
  73.3 0.0 copy-done
  73.3 0.0 copy-done.1
  73.3 6.1 %multiply_add_fusion = f32[2048,896]{0,1:T(8,128)} fusion(bf16[2048,896]{0,1:T(8,128)(2,1)} %copy.14, bf16[2048,64]{0,1:T(8,128)(2,1)S(1)} %copy-done, bf16[64,896]{1,0:T(8,128)(2,1)S(1)} %copy-done.1), kind=kOutput, calls=%fused_computation.4 | convolution fusion | flops 240386048 | bytes 11386880 | tf_op jit(solution)/shard_map/dot_general | solution.py:13
  79.4 50.5 %all-to-all-done = bf16[256,4,2048]{0,2,1:T(8,128)(2,1)} async-done(((bf16[256,4,2048]{0,2,1:T(8,128)(2,1)}), bf16[256,4,2048]{0,2,1:T(8,128)(2,1)}, u32[]{:S(2)}, u32[]{:S(2)}) %all-to-all-start) | async-done | bytes 4194336 | tf_op jit(solution)/shard_map/all_to_all | solution.py:12
  129.9 6.3 %copy.13 = bf16[4,256,2048]{2,1,0:T(8,128)(2,1)} copy(bf16[4,256,2048]{1,2,0:T(8,128)(2,1)} %bitcast.1) | data formatting | bytes 8388608 | tf_op jit(solution)/shard_map/all_to_all | solution.py:12
  136.2 12.4 %multiply_reduce_fusion = (f32[2048]{0:T(1024)S(1)}, f32[2048]{0:T(1024)S(1)}, f32[2048,896]{0,1:T(8,128)}) fusion(f32[2048,896]{0,1:T(8,128)} %multiply_add_fusion, bf16[1024,2048]{1,0:T(8,128)(2,1)} %bitcast.18, bf16[1024,896]{1,0:T(8,128)(2,1)} %all-gather.7.cloned.1.call-done), kind=kOutput, calls=%fused_computation.2 | convolution fusion | flops 3765432320 | bytes 20725760 | tf_op jit(solution)/shard_map/dot_general | solution.py:29
  148.6 120.9 %all-reduce = (f32[2048]{0:T(1024)S(1)}, f32[2048]{0:T(1024)S(1)}) all-reduce(f32[2048]{0:T(1024)S(1)} %get-tuple-element.5, f32[2048]{0:T(1024)S(1)} %get-tuple-element.4), channel_id=1, replica_groups=mesh['dp'=4,'tensor'=32] {'tensor'}, use_global_device_ids=true, to_apply=%region_1.0 | all-reduce | flops 4096 | bytes 32768 | tf_op jit(solution)/shard_map/psum | solution.py:18
  269.5 0.6 fusion.18
  270.1 10.8 %fusion.4 = f32[1024,896]{1,0:T(8,128)} fusion(bf16[1024,2048]{1,0:T(8,128)(2,1)} %bitcast.19, f32[2048]{0:T(1024)S(1)} %get-tuple-element.9, f32[2048,896]{0,1:T(8,128)} %multiply_add_fusion), kind=kOutput, calls=%fused_computation.9 | convolution fusion | flops 3766222848 | bytes 15212544 | tf_op jit(solution)/shard_map/dot_general | solution.py:23
  280.9 0.0 reduce-scatter.2.cloned.1.call-update
  280.9 0.2 all-gather.9.cloned.1.call-start
  281.2 7.0 %fusion.9 = f32[2048,64]{0,1:T(8,128)} fusion(bf16[64,896]{1,0:T(8,128)(2,1)S(1)} %copy-done.1, f32[2048,896]{0,1:T(8,128)} %get-tuple-element.10, f32[2048]{0:T(1024)S(1)} %get-tuple-element.9), kind=kOutput, calls=%fused_computation.14 | convolution fusion | flops 1411252224 | bytes 7987200 | tf_op jit(solution)/shard_map/dot_general | solution.py:44
  288.1 0.0 all-gather.9.cloned.1.call-update
  288.2 0.0 all-reduce.3.cloned.1.call-start
  288.2 8.5 %fusion.15 = f32[64,896]{1,0:T(8,128)} fusion(bf16[2048,64]{0,1:T(8,128)(2,1)S(1)} %copy-done, f32[2048,896]{0,1:T(8,128)} %get-tuple-element.10, f32[2048]{0:T(1024)S(1)} %get-tuple-element.9), kind=kOutput, calls=%fused_computation.16 | convolution fusion | flops 1411178496 | bytes 7839744 | tf_op jit(solution)/shard_map/dot_general | solution.py:37
  296.7 0.0 all-reduce.3.cloned.1.call-update
  296.7 26.0 %reduce-scatter.2.cloned.1.call-done = f32[256,896]{1,0:T(8,128)} async-done(((f32[1024,896]{1,0:T(8,128)}), f32[256,896]{1,0:T(8,128)}) %reduce-scatter.2.cloned.1.call-update) | async-done | bytes 917520 | tf_op jit(solution)/shard_map/reduce_scatter | solution.py:22
  322.8 2.0 convert_element_type.21
  324.8 36.0 %all-gather.9.cloned.1.call-done = f32[65536,64]{0,1:T(8,128)} async-done(((f32[2048,64]{0,1:T(8,128)}), f32[65536,64]{0,1:T(8,128)}) %all-gather.9.cloned.1.call-update) | async-done | bytes 16777232 | tf_op jit(solution)/shard_map/all_gather | solution.py:49
  360.8 17.7 %copy.15 = f32[8,8,32,2048]{3,2,1,0:T(8,128)} copy(f32[8,8,32,2048]{3,1,2,0:T(8,128)} %bitcast.16) | data formatting | bytes 33554432
  378.5 9.6 %bitcast_reduce_fusion = f32[2048,64]{0,1:T(8,128)} fusion(f32[8,8,32,2048]{3,2,1,0:T(8,128)} %copy.15), kind=kLoop, calls=%fused_computation | loop fusion | flops 4063232 | bytes 17301504 | tf_op jit(solution)/shard_map/reduce_sum | solution.py:49
  388.0 1.6 copy.17
  (5 shorter events, 0.0 us)
Async XLA Ops:
  8.0 65.3 %copy-start = (bf16[2048,64]{0,1:T(8,128)(2,1)S(1)}, bf16[2048,64]{0,1:T(8,128)(2,1)}, u32[]{:S(2)}) copy-start(bf16[2048,64]{0,1:T(8,128)(2,1)} %param.10) | copy-start | bytes 786436
  8.0 53.5 %all-gather.5.cloned.1.call-start = ((), (), s32[]{:S(2)}) async-start(), calls=%async_computation.2 | async-start | bytes 4325376 | tf_op jit(solution)/shard_map/all_gather | solution.py:11
  61.5 11.8 %copy-start.1 = (bf16[64,896]{1,0:T(8,128)(2,1)S(1)}, bf16[64,896]{1,0:T(8,128)(2,1)}, u32[]{:S(2)}) copy-start(bf16[64,896]{1,0:T(8,128)(2,1)} %param.9) | copy-start | bytes 344068
  61.5 68.4 %all-to-all-start = ((bf16[256,4,2048]{0,2,1:T(8,128)(2,1)}), bf16[256,4,2048]{0,2,1:T(8,128)(2,1)}, u32[]{:S(2)}, u32[]{:S(2)}) async-start(bf16[256,4,2048]{0,2,1:T(8,128)(2,1)} %bitcast.17), calls=%async_computation | async-start | bytes 8388608 | tf_op jit(solution)/shard_map/all_to_all | solution.py:12
  66.5 69.7 %all-gather.7.cloned.1.call-start = ((), (), s32[]{:S(2)}) async-start(), calls=%async_computation.4 | async-start | bytes 2293760 | tf_op jit(solution)/shard_map/all_gather | solution.py:31
  67.1 255.7 %reduce-scatter.2.cloned.1.call-start = ((), (), s32[]{:S(2)}) async-start(), calls=%async_computation.3 | async-start | bytes 4587520 | tf_op jit(solution)/shard_map/reduce_scatter | solution.py:22
  136.2 133.3 %copy-start.2 = (f32[2048]{0:T(1024)S(1)}, f32[2048]{0:T(1024)}, u32[]{:S(2)}) copy-start(f32[2048]{0:T(1024)} %param.11) | copy-start | bytes 24580
  280.9 79.9 %all-gather.9.cloned.1.call-start = ((), (), s32[]{:S(2)}) async-start(), calls=%async_computation.6 | async-start | bytes 17301504 | tf_op jit(solution)/shard_map/all_gather | solution.py:49
  288.2 99.9 %all-reduce.3.cloned.1.call-start = ((), (), s32[]{:S(2)}) async-start(), calls=%async_computation.5 | async-start | bytes 458752 | tf_op jit(solution)/shard_map/psum | solution.py:43
Sparse Core Ops, SparseCore 0:
  11.7 49.7 all-gather.4
  288.3 72.4 all-gather.8
Sparse Core Ops, SparseCore 1:
  68.6 42.3 all-gather.6
  281.0 41.7 reduce-scatter.1
  325.5 39.3 all-reduce.2
